TPU v7x, 128 devices: a whole 4x4x4 slice. The times are simulated.
128 devices in a mesh: dp: 32 (over y, z, x_hi), mp: 4 (over x_lo, core).
Axes of the slice: x: 4 (x_hi: 2, x_lo: 2; x = x_hi * 2 + x_lo), y: 4, z: 4, core: 2. Of those that a mesh axis runs over, the one named last changes fastest.
Arguments:
- tokens: bfloat16 [8192, 2048], P('dp'), may hold values from -6 to 6
- lengths: int32 [4], replicated, may hold values from 1 to 4096, 8192 in all
- w_query: float32 [2048, 2048], P('dp', 'mp')
- w_key: float32 [2048, 2048], P('dp', 'mp')
- w_value: float32 [2048, 2048], P('dp', 'mp'), may hold values from -0.125 to 0.125
- w_out: float32 [2048, 2048], P('dp', 'mp'), may hold values from -0.125 to 0.125
- w_gate: float32 [2048, 4096], P('dp', 'mp'), may hold values from -0.125 to 0.125
- w_up: float32 [2048, 4096], P('dp', 'mp'), may hold values from -0.125 to 0.125
- w_down: float32 [4096, 2048], P('dp', 'mp'), may hold values from -0.09375 to 0.09375
Outputs:
- layer_out: bfloat16 [8192, 2048], P(('dp', 'mp'))
Inputs may be any that keep to these rules, and one draw needn't show every extreme that they name: Every prompt is 1 to 4096 tokens long and one is exactly 4096; the lengths sum to 8192.
All inputs are finite; a program needn't handle non-finite values.
Results may differ from a plain program's by a relative error of at most 0.02.
The roundings to bfloat16 on the way count: a program that leaves them out, or rounds other values in their place, can miss the bound.
Values may be sent and summed in bfloat16 or wider, within the bound.
No kernel may reach another device: no remote copies, remote signals or barrier semaphores. Data moves between devices by JAX's collectives and lax.ppermute only.
A program may use at most 128 MiB of HBM per device.

v0:
```python
import jax
import jax.numpy as jnp
from jax import lax
from jax.sharding import PartitionSpec as P

HEAD = 128
epsilon = 1e-05
theta_base = 10000.0


def passed_along(value, axis, steps):
    count = lax.axis_size(axis)
    initial, last = (max(0, -steps), min(count, count - steps))
    return lax.ppermute(value, axis, [(source, source + steps) for source in range(initial, last)])


def layer_norm(rows):
    values = rows.astype(jnp.float32)
    centre = jnp.mean(values, axis=-1, keepdims=True)
    spread = jnp.mean(jnp.square(values - centre), axis=-1, keepdims=True)
    return (values - centre) * lax.rsqrt(spread + epsilon)


def prompt_coords(first, count, lengths):
    where = first + jnp.arange(count)
    ends = jnp.cumsum(lengths)
    passed = (ends[None, :] <= where[:, None]).astype(jnp.int32)
    prompt = jnp.sum(passed, axis=1)
    offset = where - jnp.sum(passed * lengths[None, :], axis=1)
    prompt = jnp.where(where < 0, -1, prompt)
    return (prompt, offset, where)


def rotate(values, offset):
    half = values.shape[-1] // 2
    freqs = jnp.power(theta_base, -jnp.arange(half, dtype=jnp.float32) * 2.0 / values.shape[-1])
    angles = offset.astype(jnp.float32)[:, None] * freqs[None, :]
    cosine = jnp.cos(angles)[:, None, :]
    sine = jnp.sin(angles)[:, None, :]
    first_half = values[..., :half]
    second_half = values[..., half:]
    return jnp.concatenate(
        [first_half * cosine - second_half * sine, second_half * cosine + first_half * sine],
        axis=-1,
    )


def row_product(left, pieces):
    block = jnp.concatenate(pieces, axis=1)
    return jnp.dot(left, block, preferred_element_type=jnp.float32)


def on_device(tokens, lengths, w_query, w_key, w_value, w_out, w_gate, w_up, w_down):
    half_type = jnp.bfloat16
    rows = tokens.shape[0]
    narrow = w_query.shape[1]
    heads_dev = narrow // HEAD
    dp_index = lax.axis_index("dp")
    mp_index = lax.axis_index("mp")
    reach = lax.axis_size("dp") // 2
    normed = layer_norm(tokens).astype(half_type)
    joined = row_product(
        normed,
        (
            lax.all_gather(w_query.astype(half_type), "dp", axis=0, tiled=True),
            lax.all_gather(w_key.astype(half_type), "dp", axis=0, tiled=True),
            lax.all_gather(w_value.astype(half_type), "dp", axis=0, tiled=True),
        ),
    )
    q_prompt, q_offset, q_where = prompt_coords(dp_index * rows, rows, lengths)
    shaped = joined.reshape(rows, 3, heads_dev, HEAD)
    query = rotate(shaped[:, 0], q_offset).astype(half_type)
    keys = rotate(shaped[:, 1], q_offset).astype(half_type)
    values = shaped[:, 2].astype(half_type)
    own_first = dp_index * rows
    own_pair = jnp.stack((keys, values))
    scale = 1.0 / HEAD**0.5

    def online_step(state, pair, first):
        accum, total, top = state
        k_prompt, k_offset, k_where = prompt_coords(first, rows, lengths)
        scores = (
            jnp.einsum("qhd,khd->hqk", query, pair[0], preferred_element_type=jnp.float32) * scale
        )
        allowed = (q_prompt[:, None] == k_prompt[None, :]) & (k_where[None, :] <= q_where[:, None])
        scores = jnp.where(allowed[None], scores, -jnp.inf)
        new_top = jnp.maximum(top, jnp.max(scores, axis=-1, keepdims=True))
        fade = jnp.exp(top - new_top)
        weights = jnp.exp(scores - new_top)
        probs = weights.astype(half_type)
        product = jnp.einsum("hqk,khd->qhd", probs, pair[1], preferred_element_type=jnp.float32)
        accum = accum * jnp.transpose(fade, (1, 0, 2)) + product
        total = total * fade + jnp.sum(weights, axis=-1, keepdims=True)
        return (accum, total, new_top)

    start_state = (
        jnp.zeros((rows, heads_dev, HEAD), jnp.float32),
        jnp.zeros((heads_dev, rows, 1), jnp.float32),
        jnp.full((heads_dev, rows, 1), -jnp.inf, jnp.float32),
    )
    state = online_step(start_state, own_pair, own_first)

    def relay_step(hop, carry):
        carried, running = carry
        carried = passed_along(carried, "dp", 1)
        first = own_first - (hop + 1) * rows
        return (carried, online_step(running, carried, first))

    unused, state = lax.fori_loop(0, reach, relay_step, (own_pair, state))
    accum, total, top = state
    context = (accum / jnp.transpose(total, (1, 0, 2))).astype(half_type).reshape(rows, narrow)
    by_rows = lax.all_gather(w_out.astype(half_type), "dp", axis=0, tiled=True)
    server_out = lax.all_to_all(by_rows, "mp", split_axis=0, concat_axis=1, tiled=True)
    partial_out = jnp.dot(context, server_out, preferred_element_type=jnp.float32)
    attended = lax.psum(partial_out.astype(jnp.bfloat16), "mp").astype(jnp.float32)
    mixed = (tokens.astype(jnp.float32) + attended).astype(half_type)
    normed_two = layer_norm(mixed).astype(half_type)
    units = w_gate.shape[1]
    gate_up = row_product(
        normed_two,
        (
            lax.all_gather(w_gate.astype(half_type), "dp", axis=0, tiled=True),
            lax.all_gather(w_up.astype(half_type), "dp", axis=0, tiled=True),
        ),
    )
    hidden = (jax.nn.silu(gate_up[:, :units]) * gate_up[:, units:]).astype(half_type)
    gathered_down = lax.all_gather(w_down.astype(half_type), "dp", axis=0, tiled=True)
    slab = rows // lax.axis_size("mp")
    server_down = lax.all_to_all(gathered_down, "mp", split_axis=0, concat_axis=1, tiled=True)
    share = lax.psum_scatter(
        jnp.dot(hidden, server_down, preferred_element_type=jnp.float32).astype(jnp.bfloat16),
        "mp",
        scatter_dimension=0,
        tiled=True,
    ).astype(jnp.float32)
    own_rows = lax.dynamic_slice_in_dim(mixed, mp_index * slab, slab, 0)
    return (own_rows.astype(jnp.float32) + share).astype(half_type)


def solution(mesh):
    in_specs = (
        P("dp", None),
        P(),
        P("dp", "mp"),
        P("dp", "mp"),
        P("dp", "mp"),
        P("dp", "mp"),
        P("dp", "mp"),
        P("dp", "mp"),
        P("dp", "mp"),
    )
    out_specs = P(("dp", "mp"), None)
    return jax.shard_map(
        on_device, mesh=mesh, in_specs=in_specs, out_specs=out_specs, check_vma=False
    )
```

profile of v0, /device:TPU:1, one launch (start us, length us, event | category | flops | bytes accessed | tf_op | source)
XLA Modules:
  0.0 904.7 jit_solution(11053108783286988303)
XLA Ops:
  17.0 66.0 %all-gather.10.cloned.1.call-done = bf16[2048,512]{1,0:T(8,128)(2,1)} async-done(((bf16[64,512]{1,0:T(8,128)(2,1)}), bf16[2048,512]{1,0:T(8,128)(2,1)}) %all-gather.10.cloned.1.call-update) | async-done | bytes 2097168 | tf_op jit(solution)/shard_map/all_gather | solution.py:66
  83.0 72.1 %all-gather.12.cloned.1.call-done = bf16[2048,512]{1,0:T(8,128)(2,1)} async-done(((bf16[64,512]{1,0:T(8,128)(2,1)}), bf16[2048,512]{1,0:T(8,128)(2,1)}) %all-gather.12.cloned.1.call-update) | async-done | bytes 2097168 | tf_op jit(solution)/shard_map/all_gather | solution.py:67
  155.2 72.1 %all-gather.8.cloned.1.call-done = bf16[2048,512]{1,0:T(8,128)(2,1)} async-done(((bf16[64,512]{1,0:T(8,128)(2,1)}), bf16[2048,512]{1,0:T(8,128)(2,1)}) %all-gather.8.cloned.1.call-update) | async-done | bytes 2097168 | tf_op jit(solution)/shard_map/all_gather | solution.py:65
  227.3 5.2 fusion.13
  236.4 62.8 %all-gather.14.cloned.1.call-done = bf16[2048,512]{1,0:T(8,128)(2,1)} async-done(((bf16[64,512]{1,0:T(8,128)(2,1)}), bf16[2048,512]{1,0:T(8,128)(2,1)}) %all-gather.14.cloned.1.call-update) | async-done | bytes 2097168 | tf_op jit(solution)/shard_map/all_gather | solution.py:112
  299.2 6.5 all-to-all-start
  305.9 281.6 %while.23 = (s32[]{:T(128)}, bf16[2,256,4,128]{3,1,2,0:T(8,128)(2,1)S(1)}, f32[256,4,128]{2,0,1:T(8,128)S(1)}, f32[4,256,1]{1,0,2:T(4,128)S(1)}, f32[4,256,1]{1,...) while((s32[]{:T(128)}, ...), condition=%wide.region_11.12_spmd.clone.clone, body=%wide.region_7.11_spmd.clone.clone.sunk | while | flops 136518656 | bytes 8333513 | solution.py:109
  305.9 2.2 collective-permute-start
  308.4 36.2 %collective-permute-done = bf16[2,256,4,128]{3,1,2,0:T(8,128)(2,1)S(1)} collective-permute-done((bf16[2,256,4,128]{3,1,2,0:T(8,128)(2,1)S(1)}, bf16[2,256,4,128]{3,1,2,0:T(8,128)(2,1)S(1)}, u32[]{:S(2)}, u32[]{:S(2)}) %collective-permute-start) | collective-permute-done | bytes 524320 | tf_op jit(solution)/shard_map/while/body/eval_jaxpr/ppermute | solution.py:14
  345.6 5.6 collective-permute-start
  351.5 14.5 %collective-permute-done = bf16[2,256,4,128]{3,1,2,0:T(8,128)(2,1)S(1)} collective-permute-done((bf16[2,256,4,128]{3,1,2,0:T(8,128)(2,1)S(1)}, bf16[2,256,4,128]{3,1,2,0:T(8,128)(2,1)S(1)}, u32[]{:S(2)}, u32[]{:S(2)}) %collective-permute-start) | collective-permute-done | bytes 524320 | tf_op jit(solution)/shard_map/while/body/eval_jaxpr/ppermute | solution.py:14
  367.1 5.7 collective-permute-start
  373.1 14.8 %collective-permute-done = bf16[2,256,4,128]{3,1,2,0:T(8,128)(2,1)S(1)} collective-permute-done((bf16[2,256,4,128]{3,1,2,0:T(8,128)(2,1)S(1)}, bf16[2,256,4,128]{3,1,2,0:T(8,128)(2,1)S(1)}, u32[]{:S(2)}, u32[]{:S(2)}) %collective-permute-start) | collective-permute-done | bytes 524320 | tf_op jit(solution)/shard_map/while/body/eval_jaxpr/ppermute | solution.py:14
  389.0 5.7 collective-permute-start
  395.0 9.3 %collective-permute-done = bf16[2,256,4,128]{3,1,2,0:T(8,128)(2,1)S(1)} collective-permute-done((bf16[2,256,4,128]{3,1,2,0:T(8,128)(2,1)S(1)}, bf16[2,256,4,128]{3,1,2,0:T(8,128)(2,1)S(1)}, u32[]{:S(2)}, u32[]{:S(2)}) %collective-permute-start) | collective-permute-done | bytes 524320 | tf_op jit(solution)/shard_map/while/body/eval_jaxpr/ppermute | solution.py:14
  405.4 5.6 collective-permute-start
  411.3 8.4 collective-permute-done
  420.7 5.6 collective-permute-start
  426.6 7.4 collective-permute-done
  435.1 5.6 collective-permute-start
  441.0 6.5 collective-permute-done
  448.5 5.6 collective-permute-start
  454.5 5.8 collective-permute-done
  461.3 6.2 collective-permute-start
  467.8 5.8 collective-permute-done
  474.7 6.2 collective-permute-start
  481.2 5.8 collective-permute-done
  488.0 6.2 collective-permute-start
  494.6 6.1 collective-permute-done
  501.7 6.5 collective-permute-start
  508.5 7.2 collective-permute-done
  516.8 6.5 collective-permute-start
  523.6 8.3 collective-permute-done
  532.9 6.5 collective-permute-start
  539.7 9.4 %collective-permute-done = bf16[2,256,4,128]{3,1,2,0:T(8,128)(2,1)S(1)} collective-permute-done((bf16[2,256,4,128]{3,1,2,0:T(8,128)(2,1)S(1)}, bf16[2,256,4,128]{3,1,2,0:T(8,128)(2,1)S(1)}, u32[]{:S(2)}, u32[]{:S(2)}) %collective-permute-start) | collective-permute-done | bytes 524320 | tf_op jit(solution)/shard_map/while/body/eval_jaxpr/ppermute | solution.py:14
  550.1 6.5 collective-permute-start
  557.0 10.5 %collective-permute-done = bf16[2,256,4,128]{3,1,2,0:T(8,128)(2,1)S(1)} collective-permute-done((bf16[2,256,4,128]{3,1,2,0:T(8,128)(2,1)S(1)}, bf16[2,256,4,128]{3,1,2,0:T(8,128)(2,1)S(1)}, u32[]{:S(2)}, u32[]{:S(2)}) %collective-permute-start) | collective-permute-done | bytes 524320 | tf_op jit(solution)/shard_map/while/body/eval_jaxpr/ppermute | solution.py:14
  568.5 6.5 collective-permute-start
  575.3 11.2 %collective-permute-done = bf16[2,256,4,128]{3,1,2,0:T(8,128)(2,1)S(1)} collective-permute-done((bf16[2,256,4,128]{3,1,2,0:T(8,128)(2,1)S(1)}, bf16[2,256,4,128]{3,1,2,0:T(8,128)(2,1)S(1)}, u32[]{:S(2)}, u32[]{:S(2)}) %collective-permute-start) | collective-permute-done | bytes 524320 | tf_op jit(solution)/shard_map/while/body/eval_jaxpr/ppermute | solution.py:14
  587.8 2.8 copy.43
  595.8 19.7 %all-to-all-start.1 = ((bf16[4,1024,512]{2,1,0:T(8,128)(2,1)}), bf16[4,1024,512]{2,1,0:T(8,128)(2,1)}, u32[]{:S(2)}, u32[]{:S(2)}) async-start(bf16[4,1024,512]{2,1,0:T(8,128)(2,1)} %bitcast.82), calls=%async_computation.1 | async-start | bytes 8388608 | tf_op jit(solution)/shard_map/all_to_all | solution.py:129
  615.4 67.1 %all-reduce.2.cloned.1.call-done = bf16[256,2048]{1,0:T(8,128)(2,1)} async-done(((bf16[256,2048]{1,0:T(8,128)(2,1)}), bf16[256,2048]{1,0:T(8,128)(2,1)}) %all-reduce.2.cloned.1.call-update) | async-done | bytes 1048592 | tf_op jit(solution)/shard_map/psum | solution.py:115
  684.6 90.4 %all-gather.16.cloned.1.call-done = bf16[2048,1024]{1,0:T(8,128)(2,1)} async-done(((bf16[64,1024]{1,0:T(8,128)(2,1)}), bf16[2048,1024]{1,0:T(8,128)(2,1)}) %all-gather.16.cloned.1.call-update) | async-done | bytes 4194320 | tf_op jit(solution)/shard_map/all_gather | solution.py:122
  775.0 82.9 %all-gather.18.cloned.1.call-done = bf16[2048,1024]{1,0:T(8,128)(2,1)} async-done(((bf16[64,1024]{1,0:T(8,128)(2,1)}), bf16[2048,1024]{1,0:T(8,128)(2,1)}) %all-gather.18.cloned.1.call-update) | async-done | bytes 4194320 | tf_op jit(solution)/shard_map/all_gather | solution.py:123
  857.9 7.2 fusion.9
  865.1 6.3 copy.44
  871.4 5.1 convolution_convert_fusion.1
  876.5 19.9 %reduce-scatter.2.cloned.1.call-done = bf16[64,2048]{1,0:T(8,128)(2,1)} async-done(((bf16[256,2048]{1,0:T(8,128)(2,1)}), bf16[64,2048]{1,0:T(8,128)(2,1)}) %reduce-scatter.2.cloned.1.call-update) | async-done | bytes 262160 | tf_op jit(solution)/shard_map/reduce_scatter | solution.py:130
  (240 shorter events, 43.3 us)
Async XLA Ops:
  6.5 9.7 %copy-start.1 = (s32[4]{0:T(128)S(1)}, s32[4]{0:T(128)}, u32[]{:S(2)}) copy-start(s32[4]{0:T(128)} %param.12) | copy-start | bytes 52
  6.5 9.0 %copy-start = (bf16[256,2048]{1,0:T(8,128)(2,1)S(1)}, bf16[256,2048]{1,0:T(8,128)(2,1)}, u32[]{:S(2)}) copy-start(bf16[256,2048]{1,0:T(8,128)(2,1)} %param.11) | copy-start | bytes 3145732
  6.5 76.5 %all-gather.10.cloned.1.call-start = ((), (), s32[]{:S(2)}) async-start(), calls=%async_computation.4 | async-start | bytes 2162688 | tf_op jit(solution)/shard_map/all_gather | solution.py:66
  8.2 147.0 %all-gather.12.cloned.1.call-start = ((), (), s32[]{:S(2)}) async-start(), calls=%async_computation.5 | async-start | bytes 2162688 | tf_op jit(solution)/shard_map/all_gather | solution.py:67
  9.8 217.5 %all-gather.8.cloned.1.call-start = ((), (), s32[]{:S(2)}) async-start(), calls=%async_computation.3 | async-start | bytes 2162688 | tf_op jit(solution)/shard_map/all_gather | solution.py:65
  11.4 287.8 %all-gather.14.cloned.1.call-start = ((), (), s32[]{:S(2)}) async-start(), calls=%async_computation.6 | async-start | bytes 2162688 | tf_op jit(solution)/shard_map/all_gather | solution.py:112
  13.0 582.8 %all-gather.20.cloned.1.call-start = ((), (), s32[]{:S(2)}) async-start(), calls=%async_computation.10 | async-start | bytes 4325376 | tf_op jit(solution)/shard_map/all_gather | solution.py:127
  299.2 288.6 %all-to-all-start = ((bf16[4,512,512]{2,1,0:T(8,128)(2,1)}), bf16[4,512,512]{2,1,0:T(8,128)(2,1)}, u32[]{:S(2)}, u32[]{:S(2)}) async-start(bf16[4,512,512]{2,1,0:T(8,128)(2,1)} %bitcast.88), calls=%async_computation | async-start | bytes 4194304 | tf_op jit(solution)/shard_map/all_to_all | solution.py:113
  305.7 376.8 %all-reduce.2.cloned.1.call-start = ((), (), s32[]{:S(2)}) async-start(), calls=%async_computation.7 | async-start | bytes 2097152 | tf_op jit(solution)/shard_map/psum | solution.py:115
  305.9 38.7 %collective-permute-start = (bf16[2,256,4,128]{3,1,2,0:T(8,128)(2,1)S(1)}, bf16[2,256,4,128]{3,1,2,0:T(8,128)(2,1)S(1)}, u32[]{:S(2)}, u32[]{:S(2)}) collective-permute-start(bf16[2,256,4,128]{3,1,2,0:T(8,128)(2,1)S(1)} %get-tuple-element.447), channel_id=1, source_target_pairs={{0,4},{4,8},{8,12},{12,16},{16,20},{20,24},{24,28},{28,32},{32,36}... | collective-permute-start | bytes 1572872 | tf_op jit(solution)/shard_map/while/body/eval_jaxpr/ppermute | solution.py:14
  345.6 20.4 %collective-permute-start = (bf16[2,256,4,128]{3,1,2,0:T(8,128)(2,1)S(1)}, bf16[2,256,4,128]{3,1,2,0:T(8,128)(2,1)S(1)}, u32[]{:S(2)}, u32[]{:S(2)}) collective-permute-start(bf16[2,256,4,128]{3,1,2,0:T(8,128)(2,1)S(1)} %get-tuple-element.447), channel_id=1, source_target_pairs={{0,4},{4,8},{8,12},{12,16},{16,20},{20,24},{24,28},{28,32},{32,36}... | collective-permute-start | bytes 1572872 | tf_op jit(solution)/shard_map/while/body/eval_jaxpr/ppermute | solution.py:14
  367.1 20.9 %collective-permute-start = (bf16[2,256,4,128]{3,1,2,0:T(8,128)(2,1)S(1)}, bf16[2,256,4,128]{3,1,2,0:T(8,128)(2,1)S(1)}, u32[]{:S(2)}, u32[]{:S(2)}) collective-permute-start(bf16[2,256,4,128]{3,1,2,0:T(8,128)(2,1)S(1)} %get-tuple-element.447), channel_id=1, source_target_pairs={{0,4},{4,8},{8,12},{12,16},{16,20},{20,24},{24,28},{28,32},{32,36}... | collective-permute-start | bytes 1572872 | tf_op jit(solution)/shard_map/while/body/eval_jaxpr/ppermute | solution.py:14
  389.0 15.3 %collective-permute-start = (bf16[2,256,4,128]{3,1,2,0:T(8,128)(2,1)S(1)}, bf16[2,256,4,128]{3,1,2,0:T(8,128)(2,1)S(1)}, u32[]{:S(2)}, u32[]{:S(2)}) collective-permute-start(bf16[2,256,4,128]{3,1,2,0:T(8,128)(2,1)S(1)} %get-tuple-element.447), channel_id=1, source_target_pairs={{0,4},{4,8},{8,12},{12,16},{16,20},{20,24},{24,28},{28,32},{32,36}... | collective-permute-start | bytes 1572872 | tf_op jit(solution)/shard_map/while/body/eval_jaxpr/ppermute | solution.py:14
  405.4 14.3 %collective-permute-start = (bf16[2,256,4,128]{3,1,2,0:T(8,128)(2,1)S(1)}, bf16[2,256,4,128]{3,1,2,0:T(8,128)(2,1)S(1)}, u32[]{:S(2)}, u32[]{:S(2)}) collective-permute-start(bf16[2,256,4,128]{3,1,2,0:T(8,128)(2,1)S(1)} %get-tuple-element.447), channel_id=1, source_target_pairs={{0,4},{4,8},{8,12},{12,16},{16,20},{20,24},{24,28},{28,32},{32,36}... | collective-permute-start | bytes 1572872 | tf_op jit(solution)/shard_map/while/body/eval_jaxpr/ppermute | solution.py:14
  420.7 13.3 %collective-permute-start = (bf16[2,256,4,128]{3,1,2,0:T(8,128)(2,1)S(1)}, bf16[2,256,4,128]{3,1,2,0:T(8,128)(2,1)S(1)}, u32[]{:S(2)}, u32[]{:S(2)}) collective-permute-start(bf16[2,256,4,128]{3,1,2,0:T(8,128)(2,1)S(1)} %get-tuple-element.447), channel_id=1, source_target_pairs={{0,4},{4,8},{8,12},{12,16},{16,20},{20,24},{24,28},{28,32},{32,36}... | collective-permute-start | bytes 1572872 | tf_op jit(solution)/shard_map/while/body/eval_jaxpr/ppermute | solution.py:14
  435.1 12.4 %collective-permute-start = (bf16[2,256,4,128]{3,1,2,0:T(8,128)(2,1)S(1)}, bf16[2,256,4,128]{3,1,2,0:T(8,128)(2,1)S(1)}, u32[]{:S(2)}, u32[]{:S(2)}) collective-permute-start(bf16[2,256,4,128]{3,1,2,0:T(8,128)(2,1)S(1)} %get-tuple-element.447), channel_id=1, source_target_pairs={{0,4},{4,8},{8,12},{12,16},{16,20},{20,24},{24,28},{28,32},{32,36}... | collective-permute-start | bytes 1572872 | tf_op jit(solution)/shard_map/while/body/eval_jaxpr/ppermute | solution.py:14
  448.5 11.7 %collective-permute-start = (bf16[2,256,4,128]{3,1,2,0:T(8,128)(2,1)S(1)}, bf16[2,256,4,128]{3,1,2,0:T(8,128)(2,1)S(1)}, u32[]{:S(2)}, u32[]{:S(2)}) collective-permute-start(bf16[2,256,4,128]{3,1,2,0:T(8,128)(2,1)S(1)} %get-tuple-element.447), channel_id=1, source_target_pairs={{0,4},{4,8},{8,12},{12,16},{16,20},{20,24},{24,28},{28,32},{32,36}... | collective-permute-start | bytes 1572872 | tf_op jit(solution)/shard_map/while/body/eval_jaxpr/ppermute | solution.py:14
  461.3 12.3 %collective-permute-start = (bf16[2,256,4,128]{3,1,2,0:T(8,128)(2,1)S(1)}, bf16[2,256,4,128]{3,1,2,0:T(8,128)(2,1)S(1)}, u32[]{:S(2)}, u32[]{:S(2)}) collective-permute-start(bf16[2,256,4,128]{3,1,2,0:T(8,128)(2,1)S(1)} %get-tuple-element.447), channel_id=1, source_target_pairs={{0,4},{4,8},{8,12},{12,16},{16,20},{20,24},{24,28},{28,32},{32,36}... | collective-permute-start | bytes 1572872 | tf_op jit(solution)/shard_map/while/body/eval_jaxpr/ppermute | solution.py:14
  474.7 12.3 %collective-permute-start = (bf16[2,256,4,128]{3,1,2,0:T(8,128)(2,1)S(1)}, bf16[2,256,4,128]{3,1,2,0:T(8,128)(2,1)S(1)}, u32[]{:S(2)}, u32[]{:S(2)}) collective-permute-start(bf16[2,256,4,128]{3,1,2,0:T(8,128)(2,1)S(1)} %get-tuple-element.447), channel_id=1, source_target_pairs={{0,4},{4,8},{8,12},{12,16},{16,20},{20,24},{24,28},{28,32},{32,36}... | collective-permute-start | bytes 1572872 | tf_op jit(solution)/shard_map/while/body/eval_jaxpr/ppermute | solution.py:14
  488.0 12.6 %collective-permute-start = (bf16[2,256,4,128]{3,1,2,0:T(8,128)(2,1)S(1)}, bf16[2,256,4,128]{3,1,2,0:T(8,128)(2,1)S(1)}, u32[]{:S(2)}, u32[]{:S(2)}) collective-permute-start(bf16[2,256,4,128]{3,1,2,0:T(8,128)(2,1)S(1)} %get-tuple-element.447), channel_id=1, source_target_pairs={{0,4},{4,8},{8,12},{12,16},{16,20},{20,24},{24,28},{28,32},{32,36}... | collective-permute-start | bytes 1572872 | tf_op jit(solution)/shard_map/while/body/eval_jaxpr/ppermute | solution.py:14
  501.7 14.0 %collective-permute-start = (bf16[2,256,4,128]{3,1,2,0:T(8,128)(2,1)S(1)}, bf16[2,256,4,128]{3,1,2,0:T(8,128)(2,1)S(1)}, u32[]{:S(2)}, u32[]{:S(2)}) collective-permute-start(bf16[2,256,4,128]{3,1,2,0:T(8,128)(2,1)S(1)} %get-tuple-element.447), channel_id=1, source_target_pairs={{0,4},{4,8},{8,12},{12,16},{16,20},{20,24},{24,28},{28,32},{32,36}... | collective-permute-start | bytes 1572872 | tf_op jit(solution)/shard_map/while/body/eval_jaxpr/ppermute | solution.py:14
  516.8 15.1 %collective-permute-start = (bf16[2,256,4,128]{3,1,2,0:T(8,128)(2,1)S(1)}, bf16[2,256,4,128]{3,1,2,0:T(8,128)(2,1)S(1)}, u32[]{:S(2)}, u32[]{:S(2)}) collective-permute-start(bf16[2,256,4,128]{3,1,2,0:T(8,128)(2,1)S(1)} %get-tuple-element.447), channel_id=1, source_target_pairs={{0,4},{4,8},{8,12},{12,16},{16,20},{20,24},{24,28},{28,32},{32,36}... | collective-permute-start | bytes 1572872 | tf_op jit(solution)/shard_map/while/body/eval_jaxpr/ppermute | solution.py:14
  532.9 16.2 %collective-permute-start = (bf16[2,256,4,128]{3,1,2,0:T(8,128)(2,1)S(1)}, bf16[2,256,4,128]{3,1,2,0:T(8,128)(2,1)S(1)}, u32[]{:S(2)}, u32[]{:S(2)}) collective-permute-start(bf16[2,256,4,128]{3,1,2,0:T(8,128)(2,1)S(1)} %get-tuple-element.447), channel_id=1, source_target_pairs={{0,4},{4,8},{8,12},{12,16},{16,20},{20,24},{24,28},{28,32},{32,36}... | collective-permute-start | bytes 1572872 | tf_op jit(solution)/shard_map/while/body/eval_jaxpr/ppermute | solution.py:14
  550.1 17.3 %collective-permute-start = (bf16[2,256,4,128]{3,1,2,0:T(8,128)(2,1)S(1)}, bf16[2,256,4,128]{3,1,2,0:T(8,128)(2,1)S(1)}, u32[]{:S(2)}, u32[]{:S(2)}) collective-permute-start(bf16[2,256,4,128]{3,1,2,0:T(8,128)(2,1)S(1)} %get-tuple-element.447), channel_id=1, source_target_pairs={{0,4},{4,8},{8,12},{12,16},{16,20},{20,24},{24,28},{28,32},{32,36}... | collective-permute-start | bytes 1572872 | tf_op jit(solution)/shard_map/while/body/eval_jaxpr/ppermute | solution.py:14
  568.5 18.0 %collective-permute-start = (bf16[2,256,4,128]{3,1,2,0:T(8,128)(2,1)S(1)}, bf16[2,256,4,128]{3,1,2,0:T(8,128)(2,1)S(1)}, u32[]{:S(2)}, u32[]{:S(2)}) collective-permute-start(bf16[2,256,4,128]{3,1,2,0:T(8,128)(2,1)S(1)} %get-tuple-element.447), channel_id=1, source_target_pairs={{0,4},{4,8},{8,12},{12,16},{16,20},{20,24},{24,28},{28,32},{32,36}... | collective-permute-start | bytes 1572872 | tf_op jit(solution)/shard_map/while/body/eval_jaxpr/ppermute | solution.py:14
  592.4 182.6 %all-gather.16.cloned.1.call-start = ((), (), s32[]{:S(2)}) async-start(), calls=%async_computation.8 | async-start | bytes 4325376 | tf_op jit(solution)/shard_map/all_gather | solution.py:122
  594.1 263.8 %all-gather.18.cloned.1.call-start = ((), (), s32[]{:S(2)}) async-start(), calls=%async_computation.9 | async-start | bytes 4325376 | tf_op jit(solution)/shard_map/all_gather | solution.py:123
  595.8 269.3 %all-to-all-start.1 = ((bf16[4,1024,512]{2,1,0:T(8,128)(2,1)}), bf16[4,1024,512]{2,1,0:T(8,128)(2,1)}, u32[]{:S(2)}, u32[]{:S(2)}) async-start(bf16[4,1024,512]{2,1,0:T(8,128)(2,1)} %bitcast.82), calls=%async_computation.1 | async-start | bytes 8388608 | tf_op jit(solution)/shard_map/all_to_all | solution.py:129
  615.4 281.0 %reduce-scatter.2.cloned.1.call-start = ((), (), s32[]{:S(2)}) async-start(), calls=%async_computation.11 | async-start | bytes 1310720 | tf_op jit(solution)/shard_map/reduce_scatter | solution.py:130
Sparse Core Ops, SparseCore 0:
  10.5 72.4 all-gather.9
  86.2 68.9 all-gather.11
  158.3 68.9 all-gather.7
  230.3 68.9 all-gather.13
  302.1 91.9 all-gather.19
  592.5 89.9 all-reduce.1
  686.1 88.8 all-gather.15
  778.5 79.3 all-gather.17
  876.7 19.7 reduce-scatter.1
where the time goes:
time: 906 us; the launch traced here: 905 us
  waiting for transfers between devices  701 us (77%)
  starting transfers between devices  120 us (13%)
  matrix products  32.3 us (4%)
  other arithmetic  24.8 us (3%)
  between operations  13.4 us (1%)
  local copies, waits for them, and re-layouts  12.3 us (1%)
    ppermute x16, waiting for transfers between devices, passed_along(): lax.ppermute(value, axis, [(source, source + steps) for source in range(i...  167 us
    ppermute x16, starting transfers between devices, passed_along(): lax.ppermute(value, axis, [(source, source + steps) for source in range(i...  93.3 us
    all_gather x1, waiting for transfers between devices, on_device(): lax.all_gather(w_gate.astype(half_type), 'dp', axis=0, tiled=True)  90.4 us
    all_gather x1, waiting for transfers between devices, on_device(): lax.all_gather(w_up.astype(half_type), 'dp', axis=0, tiled=True)  82.9 us
    all_gather x1, waiting for transfers between devices, on_device(): lax.all_gather(w_query.astype(half_type), 'dp', axis=0, tiled=True)  72.1 us
    all_gather x1, waiting for transfers between devices, on_device(): lax.all_gather(w_value.astype(half_type), 'dp', axis=0, tiled=True)  72.1 us
    psum x1, waiting for transfers between devices, on_device(): lax.psum(partial_out.astype(jnp.bfloat16), 'mp').astype(jnp.float32)  67.1 us
    all_gather x1, waiting for transfers between devices, on_device(): lax.all_gather(w_key.astype(half_type), 'dp', axis=0, tiled=True)  66 us
  transfers between devices with their start and end apart: 27, of which 24 were waited for; matrix products, arithmetic and copies ran while one was open for 6% of the time, Pallas kernels for 0%

commit v1 on v0

--- a/solution.py
+++ b/solution.py
@@ -64,7 +64,12 @@
         (
             lax.all_gather(w_query.astype(half_type), "dp", axis=0, tiled=True),
             lax.all_gather(w_key.astype(half_type), "dp", axis=0, tiled=True),
-            lax.all_gather(w_value.astype(half_type), "dp", axis=0, tiled=True),
+            jnp.concatenate(
+                lax.all_to_all(
+                    jnp.stack([w_value.astype(half_type)] * lax.axis_size("dp")), "dp", 0, 0
+                ),
+                axis=0,
+            ),
         ),
     )
     q_prompt, q_offset, q_where = prompt_coords(dp_index * rows, rows, lengths)

time: 906 us -> 851 us (0.939)
  waiting for transfers between devices: 701 us -> 635 us
  starting transfers between devices: 120 us -> 131 us
    all_gather x1 -> x0, waiting for transfers between devices: 72.1 us -> none  [on_device(): lax.all_gather(w_value.astype(half_type), 'dp', axis=0, tiled=True)]
    all_gather x1, waiting for transfers between devices: 72.1 us -> 43.1 us  [on_device(): lax.all_gather(w_query.astype(half_type), 'dp', axis=0, tiled=True)]
    all_to_all x0 -> x1, waiting for transfers between devices: none -> 28.9 us  [on_device(): lax.all_to_all(jnp.stack([w_value.astype(half_type)] * lax.axis_size('dp'...]
    all_to_all x0 -> x1, starting transfers between devices: none -> 11.5 us  [on_device(): lax.all_to_all(jnp.stack([w_value.astype(half_type)] * lax.axis_size('dp'...]
where the time goes in v1:
time: 851 us; the launch traced here: 850 us
  waiting for transfers between devices  635 us (75%)
  starting transfers between devices  131 us (15%)
  matrix products  32.3 us (4%)
  other arithmetic  22.5 us (3%)
  local copies, waits for them, and re-layouts  13.9 us (2%)
  between operations  13.7 us (2%)
    ppermute x16, waiting for transfers between devices, passed_along(): lax.ppermute(value, axis, [(source, source + steps) for source in range(i...  167 us
    ppermute x16, starting transfers between devices, passed_along(): lax.ppermute(value, axis, [(source, source + steps) for source in range(i...  93.3 us
    all_gather x1, waiting for transfers between devices, on_device(): lax.all_gather(w_gate.astype(half_type), 'dp', axis=0, tiled=True)  90.3 us
    all_gather x1, waiting for transfers between devices, on_device(): lax.all_gather(w_up.astype(half_type), 'dp', axis=0, tiled=True)  82.9 us
    all_gather x1, waiting for transfers between devices, on_device(): lax.all_gather(w_key.astype(half_type), 'dp', axis=0, tiled=True)  72.1 us
    psum x1, waiting for transfers between devices, on_device(): lax.psum(partial_out.astype(jnp.bfloat16), 'mp').astype(jnp.float32)  67.1 us
    all_gather x1, waiting for transfers between devices, on_device(): by_rows = lax.all_gather(w_out.astype(half_type), 'dp', axis=0, tiled=True)  63 us
    all_gather x1, waiting for transfers between devices, on_device(): lax.all_gather(w_query.astype(half_type), 'dp', axis=0, tiled=True)  43.1 us
  transfers between devices with their start and end apart: 27, of which 24 were waited for; matrix products, arithmetic and copies ran while one was open for 6% of the time, Pallas kernels for 0%

profile of v1, /device:TPU:1, one launch (start us, length us, event | category | flops | bytes accessed | tf_op | source)
XLA Modules:
  0.0 849.6 jit_solution(9629496919919566374)
XLA Ops:
  13.8 11.5 %all-to-all-start = ((bf16[32,64,512]{2,1,0:T(8,128)(2,1)}), bf16[32,64,512]{2,1,0:T(8,128)(2,1)S(1)}, u32[]{:S(2)}, u32[]{:S(2)}) async-start(bf16[32,64,512]{2,1,0:T(8,128)(2,1)} %stack.4), calls=%async_computation | async-start | bytes 4194304 | tf_op jit(solution)/shard_map/all_to_all | solution.py:68
  27.7 28.9 %all-to-all-done = bf16[32,64,512]{2,1,0:T(8,128)(2,1)S(1)} async-done(((bf16[32,64,512]{2,1,0:T(8,128)(2,1)}), bf16[32,64,512]{2,1,0:T(8,128)(2,1)S(1)}, u32[]{:S(2)}, u32[]{:S(2)}) %all-to-all-start) | async-done | bytes 2097184 | tf_op jit(solution)/shard_map/all_to_all | solution.py:68
  56.6 43.1 %all-gather.7.cloned.1.call-done = bf16[2048,512]{1,0:T(8,128)(2,1)} async-done(((bf16[64,512]{1,0:T(8,128)(2,1)}), bf16[2048,512]{1,0:T(8,128)(2,1)}) %all-gather.7.cloned.1.call-update) | async-done | bytes 2097168 | tf_op jit(solution)/shard_map/all_gather | solution.py:65
  99.7 72.1 %all-gather.9.cloned.1.call-done = bf16[2048,512]{1,0:T(8,128)(2,1)} async-done(((bf16[64,512]{1,0:T(8,128)(2,1)}), bf16[2048,512]{1,0:T(8,128)(2,1)}) %all-gather.9.cloned.1.call-update) | async-done | bytes 2097168 | tf_op jit(solution)/shard_map/all_gather | solution.py:66
  171.8 5.2 fusion.13
  180.9 63.0 %all-gather.11.cloned.1.call-done = bf16[2048,512]{1,0:T(8,128)(2,1)} async-done(((bf16[64,512]{1,0:T(8,128)(2,1)}), bf16[2048,512]{1,0:T(8,128)(2,1)}) %all-gather.11.cloned.1.call-update) | async-done | bytes 2097168 | tf_op jit(solution)/shard_map/all_gather | solution.py:117
  243.9 6.5 all-to-all-start.1
  250.6 281.6 %while.23 = (s32[]{:T(128)}, bf16[2,256,4,128]{3,1,2,0:T(8,128)(2,1)S(1)}, f32[256,4,128]{2,0,1:T(8,128)S(1)}, f32[4,256,1]{1,0,2:T(4,128)S(1)}, f32[4,256,1]{1,...) while((s32[]{:T(128)}, ...), condition=%wide.region_11.12_spmd.clone.clone, body=%wide.region_7.11_spmd.clone.clone.sunk | while | flops 136518656 | bytes 8333513 | solution.py:114
  253.1 36.2 %collective-permute-done = bf16[2,256,4,128]{3,1,2,0:T(8,128)(2,1)S(1)} collective-permute-done((bf16[2,256,4,128]{3,1,2,0:T(8,128)(2,1)S(1)}, bf16[2,256,4,128]{3,1,2,0:T(8,128)(2,1)S(1)}, u32[]{:S(2)}, u32[]{:S(2)}) %collective-permute-start) | collective-permute-done | bytes 524320 | tf_op jit(solution)/shard_map/while/body/eval_jaxpr/ppermute | solution.py:14
  290.3 5.6 collective-permute-start
  296.2 14.5 %collective-permute-done = bf16[2,256,4,128]{3,1,2,0:T(8,128)(2,1)S(1)} collective-permute-done((bf16[2,256,4,128]{3,1,2,0:T(8,128)(2,1)S(1)}, bf16[2,256,4,128]{3,1,2,0:T(8,128)(2,1)S(1)}, u32[]{:S(2)}, u32[]{:S(2)}) %collective-permute-start) | collective-permute-done | bytes 524320 | tf_op jit(solution)/shard_map/while/body/eval_jaxpr/ppermute | solution.py:14
  311.8 5.8 collective-permute-start
  317.8 14.8 %collective-permute-done = bf16[2,256,4,128]{3,1,2,0:T(8,128)(2,1)S(1)} collective-permute-done((bf16[2,256,4,128]{3,1,2,0:T(8,128)(2,1)S(1)}, bf16[2,256,4,128]{3,1,2,0:T(8,128)(2,1)S(1)}, u32[]{:S(2)}, u32[]{:S(2)}) %collective-permute-start) | collective-permute-done | bytes 524320 | tf_op jit(solution)/shard_map/while/body/eval_jaxpr/ppermute | solution.py:14
  333.7 5.7 collective-permute-start
  339.7 9.3 %collective-permute-done = bf16[2,256,4,128]{3,1,2,0:T(8,128)(2,1)S(1)} collective-permute-done((bf16[2,256,4,128]{3,1,2,0:T(8,128)(2,1)S(1)}, bf16[2,256,4,128]{3,1,2,0:T(8,128)(2,1)S(1)}, u32[]{:S(2)}, u32[]{:S(2)}) %collective-permute-start) | collective-permute-done | bytes 524320 | tf_op jit(solution)/shard_map/while/body/eval_jaxpr/ppermute | solution.py:14
  350.0 5.6 collective-permute-start
  355.9 8.4 collective-permute-done
  365.3 5.6 collective-permute-start
  371.2 7.4 collective-permute-done
  379.7 5.6 collective-permute-start
  385.6 6.5 collective-permute-done
  393.2 5.6 collective-permute-start
  399.1 5.8 collective-permute-done
  406.0 6.2 collective-permute-start
  412.4 5.8 collective-permute-done
  419.3 6.2 collective-permute-start
  425.8 5.8 collective-permute-done
  432.7 6.2 collective-permute-start
  439.2 6.1 collective-permute-done
  446.4 6.5 collective-permute-start
  453.2 7.2 collective-permute-done
  461.4 6.5 collective-permute-start
  468.3 8.3 collective-permute-done
  477.6 6.5 collective-permute-start
  484.4 9.4 %collective-permute-done = bf16[2,256,4,128]{3,1,2,0:T(8,128)(2,1)S(1)} collective-permute-done((bf16[2,256,4,128]{3,1,2,0:T(8,128)(2,1)S(1)}, bf16[2,256,4,128]{3,1,2,0:T(8,128)(2,1)S(1)}, u32[]{:S(2)}, u32[]{:S(2)}) %collective-permute-start) | collective-permute-done | bytes 524320 | tf_op jit(solution)/shard_map/while/body/eval_jaxpr/ppermute | solution.py:14
  494.8 6.5 collective-permute-start
  501.6 10.5 %collective-permute-done = bf16[2,256,4,128]{3,1,2,0:T(8,128)(2,1)S(1)} collective-permute-done((bf16[2,256,4,128]{3,1,2,0:T(8,128)(2,1)S(1)}, bf16[2,256,4,128]{3,1,2,0:T(8,128)(2,1)S(1)}, u32[]{:S(2)}, u32[]{:S(2)}) %collective-permute-start) | collective-permute-done | bytes 524320 | tf_op jit(solution)/shard_map/while/body/eval_jaxpr/ppermute | solution.py:14
  513.1 6.5 collective-permute-start
  519.9 11.2 %collective-permute-done = bf16[2,256,4,128]{3,1,2,0:T(8,128)(2,1)S(1)} collective-permute-done((bf16[2,256,4,128]{3,1,2,0:T(8,128)(2,1)S(1)}, bf16[2,256,4,128]{3,1,2,0:T(8,128)(2,1)S(1)}, u32[]{:S(2)}, u32[]{:S(2)}) %collective-permute-start) | collective-permute-done | bytes 524320 | tf_op jit(solution)/shard_map/while/body/eval_jaxpr/ppermute | solution.py:14
  532.4 2.8 copy.43
  540.4 19.7 %all-to-all-start.2 = ((bf16[4,1024,512]{2,1,0:T(8,128)(2,1)}), bf16[4,1024,512]{2,1,0:T(8,128)(2,1)}, u32[]{:S(2)}, u32[]{:S(2)}) async-start(bf16[4,1024,512]{2,1,0:T(8,128)(2,1)} %bitcast.83), calls=%async_computation.2 | async-start | bytes 8388608 | tf_op jit(solution)/shard_map/all_to_all | solution.py:134
  560.1 67.1 %all-reduce.2.cloned.1.call-done = bf16[256,2048]{1,0:T(8,128)(2,1)} async-done(((bf16[256,2048]{1,0:T(8,128)(2,1)}), bf16[256,2048]{1,0:T(8,128)(2,1)}) %all-reduce.2.cloned.1.call-update) | async-done | bytes 1048592 | tf_op jit(solution)/shard_map/psum | solution.py:120
  629.2 90.3 %all-gather.13.cloned.1.call-done = bf16[2048,1024]{1,0:T(8,128)(2,1)} async-done(((bf16[64,1024]{1,0:T(8,128)(2,1)}), bf16[2048,1024]{1,0:T(8,128)(2,1)}) %all-gather.13.cloned.1.call-update) | async-done | bytes 4194320 | tf_op jit(solution)/shard_map/all_gather | solution.py:127
  719.5 82.9 %all-gather.15.cloned.1.call-done = bf16[2048,1024]{1,0:T(8,128)(2,1)} async-done(((bf16[64,1024]{1,0:T(8,128)(2,1)}), bf16[2048,1024]{1,0:T(8,128)(2,1)}) %all-gather.15.cloned.1.call-update) | async-done | bytes 4194320 | tf_op jit(solution)/shard_map/all_gather | solution.py:128
  802.4 7.2 fusion.9
  809.6 6.3 copy.44
  815.9 5.1 convolution_convert_fusion.1
  821.0 20.1 %reduce-scatter.2.cloned.1.call-done = bf16[64,2048]{1,0:T(8,128)(2,1)} async-done(((bf16[256,2048]{1,0:T(8,128)(2,1)}), bf16[64,2048]{1,0:T(8,128)(2,1)}) %reduce-scatter.2.cloned.1.call-update) | async-done | bytes 262160 | tf_op jit(solution)/shard_map/reduce_scatter | solution.py:135
  (242 shorter events, 44.7 us)
Async XLA Ops:
  6.5 93.1 %all-gather.7.cloned.1.call-start = ((), (), s32[]{:S(2)}) async-start(), calls=%async_computation.4 | async-start | bytes 2162688 | tf_op jit(solution)/shard_map/all_gather | solution.py:65
  8.1 163.7 %all-gather.9.cloned.1.call-start = ((), (), s32[]{:S(2)}) async-start(), calls=%async_computation.5 | async-start | bytes 2162688 | tf_op jit(solution)/shard_map/all_gather | solution.py:66
  9.7 234.2 %all-gather.11.cloned.1.call-start = ((), (), s32[]{:S(2)}) async-start(), calls=%async_computation.6 | async-start | bytes 2162688 | tf_op jit(solution)/shard_map/all_gather | solution.py:117
  13.8 11.5 %copy-start.1 = (f32[128,512]{1,0:T(8,128)S(1)}, f32[128,512]{1,0:T(8,128)}, u32[]{:S(2)}) copy-start(f32[128,512]{1,0:T(8,128)} %param.19) | copy-start | bytes 786436
  13.8 12.3 %copy-start.2 = (s32[4]{0:T(128)S(1)}, s32[4]{0:T(128)}, u32[]{:S(2)}) copy-start(s32[4]{0:T(128)} %param.12) | copy-start | bytes 52
  13.8 12.5 %copy-start = (bf16[256,2048]{1,0:T(8,128)(2,1)S(1)}, bf16[256,2048]{1,0:T(8,128)(2,1)}, u32[]{:S(2)}) copy-start(bf16[256,2048]{1,0:T(8,128)(2,1)} %param.11) | copy-start | bytes 3145732
  13.8 42.8 %all-to-all-start = ((bf16[32,64,512]{2,1,0:T(8,128)(2,1)}), bf16[32,64,512]{2,1,0:T(8,128)(2,1)S(1)}, u32[]{:S(2)}, u32[]{:S(2)}) async-start(bf16[32,64,512]{2,1,0:T(8,128)(2,1)} %stack.4), calls=%async_computation | async-start | bytes 4194304 | tf_op jit(solution)/shard_map/all_to_all | solution.py:68
  25.3 515.2 %all-gather.17.cloned.1.call-start = ((), (), s32[]{:S(2)}) async-start(), calls=%async_computation.10 | async-start | bytes 4325376 | tf_op jit(solution)/shard_map/all_gather | solution.py:132
  243.9 288.6 %all-to-all-start.1 = ((bf16[4,512,512]{2,1,0:T(8,128)(2,1)}), bf16[4,512,512]{2,1,0:T(8,128)(2,1)}, u32[]{:S(2)}, u32[]{:S(2)}) async-start(bf16[4,512,512]{2,1,0:T(8,128)(2,1)} %bitcast.89), calls=%async_computation.1 | async-start | bytes 4194304 | tf_op jit(solution)/shard_map/all_to_all | solution.py:118
  250.4 376.8 %all-reduce.2.cloned.1.call-start = ((), (), s32[]{:S(2)}) async-start(), calls=%async_computation.7 | async-start | bytes 2097152 | tf_op jit(solution)/shard_map/psum | solution.py:120
  250.6 38.7 %collective-permute-start = (bf16[2,256,4,128]{3,1,2,0:T(8,128)(2,1)S(1)}, bf16[2,256,4,128]{3,1,2,0:T(8,128)(2,1)S(1)}, u32[]{:S(2)}, u32[]{:S(2)}) collective-permute-start(bf16[2,256,4,128]{3,1,2,0:T(8,128)(2,1)S(1)} %get-tuple-element.447), channel_id=1, source_target_pairs={{0,4},{4,8},{8,12},{12,16},{16,20},{20,24},{24,28},{28,32},{32,36}... | collective-permute-start | bytes 1572872 | tf_op jit(solution)/shard_map/while/body/eval_jaxpr/ppermute | solution.py:14
  290.3 20.4 %collective-permute-start = (bf16[2,256,4,128]{3,1,2,0:T(8,128)(2,1)S(1)}, bf16[2,256,4,128]{3,1,2,0:T(8,128)(2,1)S(1)}, u32[]{:S(2)}, u32[]{:S(2)}) collective-permute-start(bf16[2,256,4,128]{3,1,2,0:T(8,128)(2,1)S(1)} %get-tuple-element.447), channel_id=1, source_target_pairs={{0,4},{4,8},{8,12},{12,16},{16,20},{20,24},{24,28},{28,32},{32,36}... | collective-permute-start | bytes 1572872 | tf_op jit(solution)/shard_map/while/body/eval_jaxpr/ppermute | solution.py:14
  311.8 20.9 %collective-permute-start = (bf16[2,256,4,128]{3,1,2,0:T(8,128)(2,1)S(1)}, bf16[2,256,4,128]{3,1,2,0:T(8,128)(2,1)S(1)}, u32[]{:S(2)}, u32[]{:S(2)}) collective-permute-start(bf16[2,256,4,128]{3,1,2,0:T(8,128)(2,1)S(1)} %get-tuple-element.447), channel_id=1, source_target_pairs={{0,4},{4,8},{8,12},{12,16},{16,20},{20,24},{24,28},{28,32},{32,36}... | collective-permute-start | bytes 1572872 | tf_op jit(solution)/shard_map/while/body/eval_jaxpr/ppermute | solution.py:14
  333.7 15.3 %collective-permute-start = (bf16[2,256,4,128]{3,1,2,0:T(8,128)(2,1)S(1)}, bf16[2,256,4,128]{3,1,2,0:T(8,128)(2,1)S(1)}, u32[]{:S(2)}, u32[]{:S(2)}) collective-permute-start(bf16[2,256,4,128]{3,1,2,0:T(8,128)(2,1)S(1)} %get-tuple-element.447), channel_id=1, source_target_pairs={{0,4},{4,8},{8,12},{12,16},{16,20},{20,24},{24,28},{28,32},{32,36}... | collective-permute-start | bytes 1572872 | tf_op jit(solution)/shard_map/while/body/eval_jaxpr/ppermute | solution.py:14
  350.0 14.3 %collective-permute-start = (bf16[2,256,4,128]{3,1,2,0:T(8,128)(2,1)S(1)}, bf16[2,256,4,128]{3,1,2,0:T(8,128)(2,1)S(1)}, u32[]{:S(2)}, u32[]{:S(2)}) collective-permute-start(bf16[2,256,4,128]{3,1,2,0:T(8,128)(2,1)S(1)} %get-tuple-element.447), channel_id=1, source_target_pairs={{0,4},{4,8},{8,12},{12,16},{16,20},{20,24},{24,28},{28,32},{32,36}... | collective-permute-start | bytes 1572872 | tf_op jit(solution)/shard_map/while/body/eval_jaxpr/ppermute | solution.py:14
  365.3 13.3 %collective-permute-start = (bf16[2,256,4,128]{3,1,2,0:T(8,128)(2,1)S(1)}, bf16[2,256,4,128]{3,1,2,0:T(8,128)(2,1)S(1)}, u32[]{:S(2)}, u32[]{:S(2)}) collective-permute-start(bf16[2,256,4,128]{3,1,2,0:T(8,128)(2,1)S(1)} %get-tuple-element.447), channel_id=1, source_target_pairs={{0,4},{4,8},{8,12},{12,16},{16,20},{20,24},{24,28},{28,32},{32,36}... | collective-permute-start | bytes 1572872 | tf_op jit(solution)/shard_map/while/body/eval_jaxpr/ppermute | solution.py:14
  379.7 12.4 %collective-permute-start = (bf16[2,256,4,128]{3,1,2,0:T(8,128)(2,1)S(1)}, bf16[2,256,4,128]{3,1,2,0:T(8,128)(2,1)S(1)}, u32[]{:S(2)}, u32[]{:S(2)}) collective-permute-start(bf16[2,256,4,128]{3,1,2,0:T(8,128)(2,1)S(1)} %get-tuple-element.447), channel_id=1, source_target_pairs={{0,4},{4,8},{8,12},{12,16},{16,20},{20,24},{24,28},{28,32},{32,36}... | collective-permute-start | bytes 1572872 | tf_op jit(solution)/shard_map/while/body/eval_jaxpr/ppermute | solution.py:14
  393.2 11.7 %collective-permute-start = (bf16[2,256,4,128]{3,1,2,0:T(8,128)(2,1)S(1)}, bf16[2,256,4,128]{3,1,2,0:T(8,128)(2,1)S(1)}, u32[]{:S(2)}, u32[]{:S(2)}) collective-permute-start(bf16[2,256,4,128]{3,1,2,0:T(8,128)(2,1)S(1)} %get-tuple-element.447), channel_id=1, source_target_pairs={{0,4},{4,8},{8,12},{12,16},{16,20},{20,24},{24,28},{28,32},{32,36}... | collective-permute-start | bytes 1572872 | tf_op jit(solution)/shard_map/while/body/eval_jaxpr/ppermute | solution.py:14
  406.0 12.3 %collective-permute-start = (bf16[2,256,4,128]{3,1,2,0:T(8,128)(2,1)S(1)}, bf16[2,256,4,128]{3,1,2,0:T(8,128)(2,1)S(1)}, u32[]{:S(2)}, u32[]{:S(2)}) collective-permute-start(bf16[2,256,4,128]{3,1,2,0:T(8,128)(2,1)S(1)} %get-tuple-element.447), channel_id=1, source_target_pairs={{0,4},{4,8},{8,12},{12,16},{16,20},{20,24},{24,28},{28,32},{32,36}... | collective-permute-start | bytes 1572872 | tf_op jit(solution)/shard_map/while/body/eval_jaxpr/ppermute | solution.py:14
  419.3 12.3 %collective-permute-start = (bf16[2,256,4,128]{3,1,2,0:T(8,128)(2,1)S(1)}, bf16[2,256,4,128]{3,1,2,0:T(8,128)(2,1)S(1)}, u32[]{:S(2)}, u32[]{:S(2)}) collective-permute-start(bf16[2,256,4,128]{3,1,2,0:T(8,128)(2,1)S(1)} %get-tuple-element.447), channel_id=1, source_target_pairs={{0,4},{4,8},{8,12},{12,16},{16,20},{20,24},{24,28},{28,32},{32,36}... | collective-permute-start | bytes 1572872 | tf_op jit(solution)/shard_map/while/body/eval_jaxpr/ppermute | solution.py:14
  432.7 12.6 %collective-permute-start = (bf16[2,256,4,128]{3,1,2,0:T(8,128)(2,1)S(1)}, bf16[2,256,4,128]{3,1,2,0:T(8,128)(2,1)S(1)}, u32[]{:S(2)}, u32[]{:S(2)}) collective-permute-start(bf16[2,256,4,128]{3,1,2,0:T(8,128)(2,1)S(1)} %get-tuple-element.447), channel_id=1, source_target_pairs={{0,4},{4,8},{8,12},{12,16},{16,20},{20,24},{24,28},{28,32},{32,36}... | collective-permute-start | bytes 1572872 | tf_op jit(solution)/shard_map/while/body/eval_jaxpr/ppermute | solution.py:14
  446.4 14.0 %collective-permute-start = (bf16[2,256,4,128]{3,1,2,0:T(8,128)(2,1)S(1)}, bf16[2,256,4,128]{3,1,2,0:T(8,128)(2,1)S(1)}, u32[]{:S(2)}, u32[]{:S(2)}) collective-permute-start(bf16[2,256,4,128]{3,1,2,0:T(8,128)(2,1)S(1)} %get-tuple-element.447), channel_id=1, source_target_pairs={{0,4},{4,8},{8,12},{12,16},{16,20},{20,24},{24,28},{28,32},{32,36}... | collective-permute-start | bytes 1572872 | tf_op jit(solution)/shard_map/while/body/eval_jaxpr/ppermute | solution.py:14
  461.4 15.1 %collective-permute-start = (bf16[2,256,4,128]{3,1,2,0:T(8,128)(2,1)S(1)}, bf16[2,256,4,128]{3,1,2,0:T(8,128)(2,1)S(1)}, u32[]{:S(2)}, u32[]{:S(2)}) collective-permute-start(bf16[2,256,4,128]{3,1,2,0:T(8,128)(2,1)S(1)} %get-tuple-element.447), channel_id=1, source_target_pairs={{0,4},{4,8},{8,12},{12,16},{16,20},{20,24},{24,28},{28,32},{32,36}... | collective-permute-start | bytes 1572872 | tf_op jit(solution)/shard_map/while/body/eval_jaxpr/ppermute | solution.py:14
  477.6 16.2 %collective-permute-start = (bf16[2,256,4,128]{3,1,2,0:T(8,128)(2,1)S(1)}, bf16[2,256,4,128]{3,1,2,0:T(8,128)(2,1)S(1)}, u32[]{:S(2)}, u32[]{:S(2)}) collective-permute-start(bf16[2,256,4,128]{3,1,2,0:T(8,128)(2,1)S(1)} %get-tuple-element.447), channel_id=1, source_target_pairs={{0,4},{4,8},{8,12},{12,16},{16,20},{20,24},{24,28},{28,32},{32,36}... | collective-permute-start | bytes 1572872 | tf_op jit(solution)/shard_map/while/body/eval_jaxpr/ppermute | solution.py:14
  494.8 17.3 %collective-permute-start = (bf16[2,256,4,128]{3,1,2,0:T(8,128)(2,1)S(1)}, bf16[2,256,4,128]{3,1,2,0:T(8,128)(2,1)S(1)}, u32[]{:S(2)}, u32[]{:S(2)}) collective-permute-start(bf16[2,256,4,128]{3,1,2,0:T(8,128)(2,1)S(1)} %get-tuple-element.447), channel_id=1, source_target_pairs={{0,4},{4,8},{8,12},{12,16},{16,20},{20,24},{24,28},{28,32},{32,36}... | collective-permute-start | bytes 1572872 | tf_op jit(solution)/shard_map/while/body/eval_jaxpr/ppermute | solution.py:14
  513.1 18.0 %collective-permute-start = (bf16[2,256,4,128]{3,1,2,0:T(8,128)(2,1)S(1)}, bf16[2,256,4,128]{3,1,2,0:T(8,128)(2,1)S(1)}, u32[]{:S(2)}, u32[]{:S(2)}) collective-permute-start(bf16[2,256,4,128]{3,1,2,0:T(8,128)(2,1)S(1)} %get-tuple-element.447), channel_id=1, source_target_pairs={{0,4},{4,8},{8,12},{12,16},{16,20},{20,24},{24,28},{28,32},{32,36}... | collective-permute-start | bytes 1572872 | tf_op jit(solution)/shard_map/while/body/eval_jaxpr/ppermute | solution.py:14
  537.1 182.5 %all-gather.13.cloned.1.call-start = ((), (), s32[]{:S(2)}) async-start(), calls=%async_computation.8 | async-start | bytes 4325376 | tf_op jit(solution)/shard_map/all_gather | solution.py:127
  538.7 263.7 %all-gather.15.cloned.1.call-start = ((), (), s32[]{:S(2)}) async-start(), calls=%async_computation.9 | async-start | bytes 4325376 | tf_op jit(solution)/shard_map/all_gather | solution.py:128
  540.4 269.2 %all-to-all-start.2 = ((bf16[4,1024,512]{2,1,0:T(8,128)(2,1)}), bf16[4,1024,512]{2,1,0:T(8,128)(2,1)}, u32[]{:S(2)}, u32[]{:S(2)}) async-start(bf16[4,1024,512]{2,1,0:T(8,128)(2,1)} %bitcast.83), calls=%async_computation.2 | async-start | bytes 8388608 | tf_op jit(solution)/shard_map/all_to_all | solution.py:134
  560.1 281.0 %reduce-scatter.2.cloned.1.call-start = ((), (), s32[]{:S(2)}) async-start(), calls=%async_computation.11 | async-start | bytes 1310720 | tf_op jit(solution)/shard_map/reduce_scatter | solution.py:135
Sparse Core Ops, SparseCore 0:
  10.5 89.1 all-gather.6
  102.8 68.9 all-gather.8
  174.9 68.9 all-gather.10
  246.8 91.9 all-gather.16
  537.2 89.9 all-reduce.1
  630.6 88.8 all-gather.12
  723.0 79.3 all-gather.14
  821.1 19.9 reduce-scatter.1
